TPU v7x, 512 devices: a whole 4x4x16 slice. The times are simulated.
512 devices in a mesh: dp: 8 (over x, core), tensor: 64 (over z, y).
Axes of the slice: x: 4, y: 4, z: 16, core: 2. Of those that a mesh axis runs over, the one named last changes fastest.
Arguments:
- states: bfloat16 [65536, 2048], P(('dp', 'tensor')), may hold values from -150 to 150
- norm_gain: float32 [2048], replicated, may hold values from 0.1 to 1.9
- norm_bias: float32 [2048], replicated, may hold values from -3 to 3
- head_table: bfloat16 [250880, 2048], P('tensor', 'dp'), may hold values from -2 to 2
- seq_lengths: int32 [8], P('dp'), may hold values from 4096 to 8192
- scored_index: int32 [2048], P('dp'), may hold values from 0 to 8191
- targets: int32 [2048], P('dp'), may hold values from 0 to 250879
- slot_mask: int32 [2048], P('dp'), may hold values 0 or 1
Outputs:
- logprob: float32 [2048], P(('dp', 'tensor'))
- entropy: float32 [2048], P(('dp', 'tensor'))
All inputs are finite; a program needn't handle non-finite values. No bound on the sum of `slot_mask` on one device may be relied on, other than what follows from the above.
Results may differ from a plain program's by a relative error of at most 0.012.
The roundings to bfloat16 on the way count: a program that leaves them out, or rounds other values in their place, can miss the bound.
Values may be sent and summed in bfloat16 or wider, within the bound.
No kernel may reach another device: no remote copies, remote signals or barrier semaphores. Data moves between devices by JAX's collectives and lax.ppermute only.
A program may use at most 64 MiB of HBM per device.

v0:
```python
import jax
import jax.numpy as jnp
from jax import lax
from jax.sharding import Mesh, PartitionSpec as P

EPSILON = 1e-05
TENSOR = ("tz", "ty")


def layer_norm(states, norm_gain, norm_bias):
    values = states.astype(jnp.float32)
    center = jnp.mean(values, axis=1, keepdims=True)
    shifted = values - center
    variance = jnp.mean(shifted * shifted, axis=1, keepdims=True)
    return (shifted * lax.rsqrt(variance + EPSILON) * norm_gain + norm_bias).astype(jnp.bfloat16)


def contract_last(left, right):
    return lax.dot_general(
        left, right, (((1,), (1,)), ((), ())), preferred_element_type=jnp.float32
    )


def body(states, norm_gain, norm_bias, head_table, seq_lengths, scored_index, targets, slot_mask):
    local_rows = states.shape[0]
    devices = lax.axis_size(TENSOR)
    position = lax.axis_index(TENSOR)
    first_row = position * local_rows
    scored_count = scored_index.shape[0]
    owned_count = scored_count // devices
    offset = position * owned_count
    width = states.shape[1]
    row_iota = jnp.arange(local_rows, dtype=jnp.int32)
    picker = (scored_index[:, None] - first_row == row_iota[None, :]).astype(jnp.bfloat16)
    picked = jnp.dot(picker, states, preferred_element_type=jnp.float32).astype(jnp.bfloat16)
    ring = lax.axis_size("ty")
    by_y = picked.reshape(devices // ring, ring, owned_count, width).transpose(1, 0, 2, 3)
    near = lax.all_to_all(by_y, "ty", 0, 0, tiled=True)
    near = jnp.sum(near.astype(jnp.float32), axis=0).astype(jnp.bfloat16)
    arrived = lax.all_to_all(near, "tz", 0, 0, tiled=True)
    owned_rows = jnp.sum(arrived.astype(jnp.float32), axis=0)
    owned_normed = layer_norm(owned_rows, norm_gain, norm_bias)
    along_z = lax.all_to_all(
        jnp.broadcast_to(owned_normed[None], (devices // ring, owned_count, width)),
        "tz",
        0,
        0,
        tiled=True,
    )
    along_y = lax.all_to_all(
        jnp.broadcast_to(along_z[None], (ring, devices // ring, owned_count, width)),
        "ty",
        0,
        0,
        tiled=True,
    )
    chosen = along_y.transpose(1, 0, 2, 3).reshape(scored_count, width)
    vocab_local = head_table.shape[0]
    split = vocab_local // 32 * 16
    local_target = targets - position * vocab_local
    parts = []
    for low, high in ((0, split), (split, vocab_local)):
        logits = contract_last(
            chosen, lax.all_gather(head_table[low:high], "dp", axis=1, tiled=True)
        )
        vocab_iota = jnp.arange(low, high, dtype=jnp.int32)
        target_hits = local_target[:, None] == vocab_iota[None, :]
        part_maxima = jnp.max(logits, axis=1)
        shifted = logits - part_maxima[:, None]
        weights = jnp.exp(shifted)
        parts.append(
            jnp.stack(
                [
                    part_maxima,
                    jnp.sum(weights, axis=1),
                    jnp.sum(weights * shifted, axis=1),
                    jnp.sum(jnp.where(target_hits, logits, 0.0), axis=1),
                ],
                axis=1,
            )
        )
    stats = jnp.stack(parts, axis=1)
    gathered = lax.all_to_all(stats.reshape(devices, owned_count, 2, 4), TENSOR, 0, 0, tiled=True)
    gathered = gathered.transpose(0, 2, 1, 3).reshape(devices * 2, owned_count, 4)
    part_max = gathered[:, :, 0]
    maxima = jnp.max(part_max, axis=0)
    gap = part_max - maxima[None, :]
    scale = jnp.exp(gap)
    totals = jnp.sum(scale * gathered[:, :, 1], axis=0)
    weighted = jnp.sum(scale * (gathered[:, :, 2] + gap * gathered[:, :, 1]), axis=0)
    target_logit = jnp.sum(gathered[:, :, 3], axis=0)
    own_index = lax.dynamic_slice_in_dim(scored_index, offset, owned_count)
    own_mask = lax.dynamic_slice_in_dim(slot_mask, offset, owned_count)
    segment = local_rows * devices // seq_lengths.shape[0]
    sequence = own_index // segment
    seq_iota = jnp.arange(seq_lengths.shape[0], dtype=jnp.int32)
    length_of = jnp.sum(
        jnp.where(sequence[:, None] == seq_iota[None, :], seq_lengths[None, :], 0), axis=1
    )
    live_slot = (own_mask == 1) & (own_index % segment < length_of)
    log_total = jnp.log(totals)
    logprob = jnp.where(live_slot, target_logit - maxima - log_total, 0.0)
    entropy = jnp.where(live_slot, log_total - weighted / totals, 0.0)
    return (logprob, entropy)


def split_mesh(mesh):
    grid = mesh.devices
    first = grid[0]
    coords = [getattr(d, "coords", None) for d in first]
    ring = len({c[1] for c in coords}) if all((c is not None for c in coords)) else 1
    return Mesh(grid.reshape(grid.shape[0], grid.shape[1] // ring, ring), ("dp", "tz", "ty"))


def solution(mesh):
    return jax.shard_map(
        body,
        mesh=split_mesh(mesh),
        in_specs=(
            P(("dp", "tz", "ty"), None),
            P(),
            P(),
            P(("tz", "ty"), "dp"),
            P("dp"),
            P("dp"),
            P("dp"),
            P("dp"),
        ),
        out_specs=(P(("dp", "tz", "ty")), P(("dp", "tz", "ty"))),
        check_vma=False,
    )
```

profile of v0, /device:TPU:2, one launch (start us, length us, event | category | flops | bytes accessed | tf_op | source)
XLA Modules:
  0.0 195.1 jit_solution(13988544709984714789)
XLA Ops:
  7.2 2.4 %slice.19 = bf16[1952,256]{1,0:T(8,128)(2,1)} slice(bf16[3920,256]{1,0:T(8,128)(2,1)} %param.11), slice={[0:1952], [0:256]} | slice | bytes 1998848 | tf_op jit(solution)/shard_map/slice | solution.py:64
  9.7 1.0 slice.20
  10.8 0.5 convolution_convert_fusion
  11.3 0.4 reshape.125
  11.7 0.5 copy.70
  12.2 19.4 %all_to_all.25 = bf16[4,16,4,2048]{3,2,1,0:T(4,128)(2,1)S(1)} all-to-all(bf16[4,16,4,2048]{3,2,1,0:T(4,128)(2,1)S(1)} %bitcast.15), channel_id=1, replica_groups=mesh['dp'=8,'tz'=16,'ty'=4] {'ty'}, dimensions={0} | all-to-all | bytes 2097152 | tf_op jit(solution)/shard_map/all_to_all | solution.py:38
  31.6 0.7 reduce_sum.124
  32.3 32.5 %all_to_all.26 = bf16[16,4,2048]{2,1,0:T(4,128)(2,1)S(1)} all-to-all(bf16[16,4,2048]{2,1,0:T(4,128)(2,1)S(1)} %reduce_sum.124), channel_id=1, replica_groups=mesh['dp'=8,'tz'=16,'ty'=4] {'tz'}, dimensions={0} | all-to-all | bytes 524288 | tf_op jit(solution)/shard_map/all_to_all | solution.py:40
  64.9 0.4 convert_reduce_fusion
  65.3 0.2 multiply_reduce_fusion
  65.7 22.5 %all_to_all.27 = bf16[16,4,2048]{2,1,0:T(4,128)(2,1)S(1)} all-to-all(bf16[16,4,2048]{2,1,0:T(4,128)(2,1)S(1)} %broadcast_in_dim.26), channel_id=1, replica_groups=mesh['dp'=8,'tz'=16,'ty'=4] {'tz'}, dimensions={0} | all-to-all | bytes 524288 | tf_op jit(solution)/shard_map/all_to_all | solution.py:43
  88.2 1.5 broadcast_in_dim.27
  89.7 3.5 %all-to-all-start.3 = ((bf16[4,16,4,2048]{3,2,1,0:T(4,128)(2,1)}), bf16[4,16,4,2048]{3,2,1,0:T(4,128)(2,1)S(1)}, u32[]{:S(2)}, u32[]{:S(2)}) async-start(bf16[4,16,4,2048]{3,2,1,0:T(4,128)(2,1)} %broadcast_in_dim.27), calls=%async_computation.3 | async-start | bytes 2097152 | tf_op jit(solution)/shard_map/all_to_all | solution.py:50
  93.2 10.8 %all-to-all-done.3 = bf16[4,16,4,2048]{3,2,1,0:T(4,128)(2,1)S(1)} async-done(((bf16[4,16,4,2048]{3,2,1,0:T(4,128)(2,1)}), bf16[4,16,4,2048]{3,2,1,0:T(4,128)(2,1)S(1)}, u32[]{:S(2)}, u32[]{:S(2)}) %all-to-all-start.3) | async-done | bytes 1048608 | tf_op jit(solution)/shard_map/all_to_all | solution.py:50
  104.0 0.6 copy.56
  104.6 1.1 reshape.126
  105.7 6.0 %fusion.4 = (f32[256]{0:T(256)S(1)}, f32[256,1952]{0,1:T(8,128)S(1)}) fusion(bf16[256,2048]{1,0:T(8,128)(2,1)} %reshape.126, bf16[1952,2048]{1,0:T(8,128)(2,1)} %all-gather.3.cloned.1.call-done), kind=kOutput, calls=%fused_computation.40 | convolution fusion | flops 2047319808 | bytes 11043840 | tf_op jit(solution)/shard_map/dot_general | solution.py:19
  111.9 0.7 exponential_reduce_fusion.1
  112.7 0.1 stack.37
  113.2 24.7 %all-gather.5.cloned.1.call-done = bf16[1968,2048]{1,0:T(8,128)(2,1)} async-done(((bf16[1968,256]{1,0:T(8,128)(2,1)}), bf16[1968,2048]{1,0:T(8,128)(2,1)}) %all-gather.5.cloned.1.call-update) | async-done | bytes 8060944 | tf_op jit(solution)/shard_map/all_gather | solution.py:64
  137.9 6.1 %fusion.3 = (f32[256]{0:T(256)S(1)}, f32[256,1968]{0,1:T(8,128)S(1)}) fusion(bf16[256,2048]{1,0:T(8,128)(2,1)} %reshape.126, bf16[1968,2048]{1,0:T(8,128)(2,1)} %all-gather.5.cloned.1.call-done), kind=kOutput, calls=%fused_computation.39 | convolution fusion | flops 2064101120 | bytes 11125760 | tf_op jit(solution)/shard_map/dot_general | solution.py:19
  144.1 1.0 exponential_reduce_fusion
  145.3 0.1 stack.42
  145.5 0.1 stack.41
  145.8 0.9 copy.65
  146.7 15.6 %all-to-all-start.4 = ((f32[64,4,2,4]{1,3,2,0:T(4,128)}), f32[64,4,2,4]{1,3,2,0:T(4,128)S(1)}, u32[]{:S(2)}, u32[]{:S(2)}) async-start(f32[64,4,2,4]{1,3,2,0:T(4,128)} %copy.65), calls=%async_computation.4 | async-start | bytes 524288 | tf_op jit(solution)/shard_map/all_to_all | solution.py:83
  163.0 22.3 %all-to-all-done.4 = f32[64,4,2,4]{1,3,2,0:T(4,128)S(1)} async-done(((f32[64,4,2,4]{1,3,2,0:T(4,128)}), f32[64,4,2,4]{1,3,2,0:T(4,128)S(1)}, u32[]{:S(2)}, u32[]{:S(2)}) %all-to-all-start.4) | async-done | bytes 8224 | tf_op jit(solution)/shard_map/all_to_all | solution.py:83
  185.3 1.0 copy.66
  186.3 0.6 slice_reduce_fusion
  186.9 0.2 multiply_reduce_fusion.1
  187.1 0.6 subtract_select_fusion
  187.7 0.5 subtract_select_fusion.1
  (40 shorter events, 1.5 us)
Async XLA Ops:
  7.2 3.7 %copy-start = (bf16[128,2048]{1,0:T(8,128)(2,1)S(1)}, bf16[128,2048]{1,0:T(8,128)(2,1)}, u32[]{:S(2)}) copy-start(bf16[128,2048]{1,0:T(8,128)(2,1)} %param.8) | copy-start | bytes 1572868
  7.2 2.5 %copy-start.1 = (bf16[3920,256]{1,0:T(8,128)(2,1)S(1)}, bf16[3920,256]{1,0:T(8,128)(2,1)}, u32[]{:S(2)}) copy-start(bf16[3920,256]{1,0:T(8,128)(2,1)} %param.11) | copy-start | bytes 6021124
  7.2 98.6 %all-gather.3.cloned.1.call-start = ((), (), s32[]{:S(2)}) async-start(), calls=%async_computation.5 | async-start | bytes 8994816 | tf_op jit(solution)/shard_map/all_gather | solution.py:64
  9.6 1.2 copy-start.4
  9.7 128.2 %all-gather.5.cloned.1.call-start = ((), (), s32[]{:S(2)}) async-start(), calls=%async_computation.6 | async-start | bytes 9068544 | tf_op jit(solution)/shard_map/all_gather | solution.py:64
  12.2 53.3 %copy-start.2 = (f32[2048]{0:T(1024)S(1)}, f32[2048]{0:T(1024)}, u32[]{:S(2)}) copy-start(f32[2048]{0:T(1024)} %param.10) | copy-start | bytes 24580
  12.2 53.3 %copy-start.3 = (f32[2048]{0:T(1024)S(1)}, f32[2048]{0:T(1024)}, u32[]{:S(2)}) copy-start(f32[2048]{0:T(1024)} %param.9) | copy-start | bytes 24580
  65.7 27.5 %copy-start.5 = (s32[256]{0:T(256)S(1)}, s32[256]{0:T(256)}, u32[]{:S(2)}) copy-start(s32[256]{0:T(256)} %param.14) | copy-start | bytes 3076
  89.7 14.4 %all-to-all-start.3 = ((bf16[4,16,4,2048]{3,2,1,0:T(4,128)(2,1)}), bf16[4,16,4,2048]{3,2,1,0:T(4,128)(2,1)S(1)}, u32[]{:S(2)}, u32[]{:S(2)}) async-start(bf16[4,16,4,2048]{3,2,1,0:T(4,128)(2,1)} %broadcast_in_dim.27), calls=%async_computation.3 | async-start | bytes 2097152 | tf_op jit(solution)/shard_map/all_to_all | solution.py:50
  144.1 43.1 %copy-start.6 = (s32[256]{0:T(256)S(1)}, s32[256]{0:T(256)}, u32[]{:S(2)}) copy-start(s32[256]{0:T(256)} %param.15) | copy-start | bytes 3076
  146.7 38.6 %all-to-all-start.4 = ((f32[64,4,2,4]{1,3,2,0:T(4,128)}), f32[64,4,2,4]{1,3,2,0:T(4,128)S(1)}, u32[]{:S(2)}, u32[]{:S(2)}) async-start(f32[64,4,2,4]{1,3,2,0:T(4,128)} %copy.65), calls=%async_computation.4 | async-start | bytes 524288 | tf_op jit(solution)/shard_map/all_to_all | solution.py:83
Sparse Core Ops, SparseCore 0:
  10.1 64.3 all-gather.2
  76.6 61.1 all-gather.4
where the time goes:
time: 196 us; the launch traced here: 195 us
  blocking collectives  74.4 us (38%)
  waiting for transfers between devices  57.8 us (29%)
  starting transfers between devices  19.2 us (10%)
  between operations  15 us (8%)
  matrix products  12.6 us (6%)
  local copies, waits for them, and re-layouts  11 us (6%)
  other arithmetic  5.14 us (3%)
    all_to_all x1, blocking collectives, body(): arrived = lax.all_to_all(near, 'tz', 0, 0, tiled=True)  32.5 us
    all_gather x2, waiting for transfers between devices, body(): lax.all_gather(head_table[low:high], 'dp', axis=1, tiled=True)  24.7 us
    all_to_all x1, blocking collectives, body(): lax.all_to_all(jnp.broadcast_to(owned_normed[None], (devices // ring, own...  22.5 us
    all_to_all x1, waiting for transfers between devices, body(): lax.all_to_all(stats.reshape(devices, owned_count, 2, 4), TENSOR, 0, 0, t...  22.3 us
    all_to_all x1, blocking collectives, body(): near = lax.all_to_all(by_y, 'ty', 0, 0, tiled=True)  19.4 us
    all_to_all x1, starting transfers between devices, body(): lax.all_to_all(stats.reshape(devices, owned_count, 2, 4), TENSOR, 0, 0, t...  15.6 us
    dot_general x2, matrix products, contract_last(): lax.dot_general(left, right, (((1,), (1,)), ((), ())), preferred_element_...  12.1 us
    all_to_all x1, waiting for transfers between devices, body(): lax.all_to_all(jnp.broadcast_to(along_z[None], (ring, devices // ring, ow...  10.8 us
  transfers between devices with their start and end apart: 4, of which 3 were waited for; matrix products, arithmetic and copies ran while one was open for 7% of the time, Pallas kernels for 0%

commit v1 on v0

--- a/solution.py
+++ b/solution.py
@@ -61,7 +61,11 @@
     parts = []
     for low, high in ((0, split), (split, vocab_local)):
         logits = contract_last(
-            chosen, lax.all_gather(head_table[low:high], "dp", axis=1, tiled=True)
+            chosen,
+            jnp.concatenate(
+                lax.all_to_all(jnp.stack([head_table[low:high]] * lax.axis_size("dp")), "dp", 0, 0),
+                axis=1,
+            ),
         )
         vocab_iota = jnp.arange(low, high, dtype=jnp.int32)
         target_hits = local_target[:, None] == vocab_iota[None, :]

time: 196 us -> 345 us (1.76)
  waiting for transfers between devices: 57.8 us -> 195 us
  local copies, waits for them, and re-layouts: 11 us -> 30.6 us
  between operations: 15 us -> 1.54 us
  starting transfers between devices: 19.2 us -> 25.2 us
    all_to_all x0 -> x2, waiting for transfers between devices: none -> 162 us  [body(): lax.all_to_all(jnp.stack([head_table[low:high]] * lax.axis_size('dp')), '...]
    all_gather x2 -> x0, waiting for transfers between devices: 24.7 us -> none  [body(): lax.all_gather(head_table[low:high], 'dp', axis=1, tiled=True)]
    reshape x0 -> x2, local copies, waits for them, and re-layouts: none -> 15.4 us  [body(): jnp.concatenate(lax.all_to_all(jnp.stack([head_table[low:high]] * lax.axi...]
    all_to_all x0 -> x2, starting transfers between devices: none -> 11.7 us  [body(): lax.all_to_all(jnp.stack([head_table[low:high]] * lax.axis_size('dp')), '...]
    another operation x0 -> x2, local copies, waits for them, and re-layouts: none -> 7.32 us  [body(): jnp.stack([head_table[low:high]] * lax.axis_size('dp'))]
    all_to_all x1, starting transfers between devices: 15.6 us -> 9.9 us  [body(): lax.all_to_all(stats.reshape(devices, owned_count, 2, 4), TENSOR, 0, 0, t...]
  transfers between devices with their start and end apart: 4 -> 4, of which waited for: 3 -> 4; matrix products, arithmetic and copies ran while one was open for 7% -> 5% of each run, Pallas kernels for 0% -> 0%
where the time goes in v1:
time: 345 us; the launch traced here: 344 us
  waiting for transfers between devices  195 us (57%)
  blocking collectives  74.3 us (22%)
  local copies, waits for them, and re-layouts  30.6 us (9%)
  starting transfers between devices  25.2 us (7%)
  matrix products  11.6 us (3%)
  other arithmetic  5.83 us (2%)
    all_to_all x2, waiting for transfers between devices, body(): lax.all_to_all(jnp.stack([head_table[low:high]] * lax.axis_size('dp')), '...  162 us
    all_to_all x1, blocking collectives, body(): arrived = lax.all_to_all(near, 'tz', 0, 0, tiled=True)  32.5 us
    all_to_all x1, blocking collectives, body(): lax.all_to_all(jnp.broadcast_to(owned_normed[None], (devices // ring, own...  22.5 us
    all_to_all x1, waiting for transfers between devices, body(): lax.all_to_all(stats.reshape(devices, owned_count, 2, 4), TENSOR, 0, 0, t...  21.7 us
    all_to_all x1, blocking collectives, body(): near = lax.all_to_all(by_y, 'ty', 0, 0, tiled=True)  19.4 us
    reshape x2, local copies, waits for them, and re-layouts, body(): jnp.concatenate(lax.all_to_all(jnp.stack([head_table[low:high]] * lax.axi...  15.4 us
    all_to_all x2, starting transfers between devices, body(): lax.all_to_all(jnp.stack([head_table[low:high]] * lax.axis_size('dp')), '...  11.7 us
    dot_general x2, matrix products, contract_last(): lax.dot_general(left, right, (((1,), (1,)), ((), ())), preferred_element_...  11.2 us
  transfers between devices with their start and end apart: 4, of which 4 were waited for; matrix products, arithmetic and copies ran while one was open for 5% of the time, Pallas kernels for 0%

profile of v1, /device:TPU:2, one launch (start us, length us, event | category | flops | bytes accessed | tf_op | source)
XLA Modules:
  0.0 344.2 jit_solution(10715193880713658785)
XLA Ops:
  0.7 0.7 broadcast_subtract_fusion.1
  1.7 0.5 convolution_convert_fusion
  2.2 0.4 reshape.141
  2.6 0.5 copy.80
  3.1 19.4 %all_to_all.35 = bf16[4,16,4,2048]{3,2,1,0:T(4,128)(2,1)S(1)} all-to-all(bf16[4,16,4,2048]{3,2,1,0:T(4,128)(2,1)S(1)} %bitcast.23), channel_id=1, replica_groups=mesh['dp'=8,'tz'=16,'ty'=4] {'ty'}, dimensions={0} | all-to-all | bytes 2097152 | tf_op jit(solution)/shard_map/all_to_all | solution.py:38
  22.4 0.7 reduce_sum.124
  23.1 32.5 %all_to_all.36 = bf16[16,4,2048]{2,1,0:T(4,128)(2,1)S(1)} all-to-all(bf16[16,4,2048]{2,1,0:T(4,128)(2,1)S(1)} %reduce_sum.124), channel_id=1, replica_groups=mesh['dp'=8,'tz'=16,'ty'=4] {'tz'}, dimensions={0} | all-to-all | bytes 524288 | tf_op jit(solution)/shard_map/all_to_all | solution.py:40
  56.5 22.5 %all_to_all.37 = bf16[16,4,2048]{2,1,0:T(4,128)(2,1)S(1)} all-to-all(bf16[16,4,2048]{2,1,0:T(4,128)(2,1)S(1)} %broadcast_in_dim.26), channel_id=1, replica_groups=mesh['dp'=8,'tz'=16,'ty'=4] {'tz'}, dimensions={0} | all-to-all | bytes 524288 | tf_op jit(solution)/shard_map/all_to_all | solution.py:43
  78.9 1.5 broadcast_in_dim.27
  80.4 3.6 %all-to-all-start.3 = ((bf16[4,16,4,2048]{3,2,1,0:T(4,128)(2,1)}), bf16[4,16,4,2048]{3,2,1,0:T(4,128)(2,1)S(1)}, u32[]{:S(2)}, u32[]{:S(2)}) async-start(bf16[4,16,4,2048]{3,2,1,0:T(4,128)(2,1)} %broadcast_in_dim.27), calls=%async_computation.3 | async-start | bytes 2097152 | tf_op jit(solution)/shard_map/all_to_all | solution.py:50
  84.1 10.9 %all-to-all-done.3 = bf16[4,16,4,2048]{3,2,1,0:T(4,128)(2,1)S(1)} async-done(((bf16[4,16,4,2048]{3,2,1,0:T(4,128)(2,1)}), bf16[4,16,4,2048]{3,2,1,0:T(4,128)(2,1)S(1)}, u32[]{:S(2)}, u32[]{:S(2)}) %all-to-all-start.3) | async-done | bytes 1048608 | tf_op jit(solution)/shard_map/all_to_all | solution.py:50
  95.0 3.6 %stack.26 = bf16[8,1952,256]{2,1,0:T(8,128)(2,1)} broadcast(bf16[1952,256]{1,0:T(8,128)(2,1)S(1)} %slice-done), dimensions={1,2} | broadcast | bytes 8994816 | tf_op jit(solution)/shard_map/stack | solution.py:66
  98.6 5.3 %all-to-all-start.4 = ((bf16[8,1952,256]{2,1,0:T(8,128)(2,1)}), bf16[8,1952,256]{2,1,0:T(8,128)(2,1)}, u32[]{:S(2)}, u32[]{:S(2)}) async-start(bf16[8,1952,256]{2,1,0:T(8,128)(2,1)} %stack.26), calls=%async_computation.4 | async-start | bytes 15990784 | tf_op jit(solution)/shard_map/all_to_all | solution.py:66
  103.9 89.1 %all-to-all-done.4 = bf16[8,1952,256]{2,1,0:T(8,128)(2,1)} async-done(((bf16[8,1952,256]{2,1,0:T(8,128)(2,1)}), bf16[8,1952,256]{2,1,0:T(8,128)(2,1)}, u32[]{:S(2)}, u32[]{:S(2)}) %all-to-all-start.4) | async-done | bytes 7995424 | tf_op jit(solution)/shard_map/all_to_all | solution.py:66
  193.0 3.7 %stack.63 = bf16[8,1968,256]{2,1,0:T(8,128)(2,1)} broadcast(bf16[1968,256]{1,0:T(8,128)(2,1)S(1)} %slice-done.1), dimensions={1,2} | broadcast | bytes 9068544 | tf_op jit(solution)/shard_map/stack | solution.py:66
  196.7 6.4 %all-to-all-start.5 = ((bf16[8,1968,256]{2,1,0:T(8,128)(2,1)}), bf16[8,1968,256]{2,1,0:T(8,128)(2,1)}, u32[]{:S(2)}, u32[]{:S(2)}) async-start(bf16[8,1968,256]{2,1,0:T(8,128)(2,1)} %stack.63), calls=%async_computation.5 | async-start | bytes 16121856 | tf_op jit(solution)/shard_map/all_to_all | solution.py:66
  203.1 0.6 copy.62
  203.7 1.1 reshape.142
  204.8 7.7 %copy.75 = bf16[8,244,8,256]{3,2,0,1:T(8,128)(2,1)} copy(bf16[8,244,8,256]{3,2,1,0:T(8,128)(2,1)} %bitcast.7) | data formatting | bytes 15990784 | tf_op jit(solution)/shard_map/reshape | solution.py:65
  212.5 5.6 %fusion.4 = (f32[256]{0:T(256)S(1)}, f32[256,1952]{0,1:T(8,128)S(1)}) fusion(bf16[256,2048]{1,0:T(8,128)(2,1)S(1)} %copy-done.2, bf16[1952,2048]{1,0:T(8,128)(2,1)} %bitcast.20), kind=kOutput, calls=%fused_computation.40 | convolution fusion | flops 2047319808 | bytes 11043840 | tf_op jit(solution)/shard_map/dot_general | solution.py:19
  218.2 0.7 exponential_reduce_fusion.1
  219.5 73.4 %all-to-all-done.5 = bf16[8,1968,256]{2,1,0:T(8,128)(2,1)} async-done(((bf16[8,1968,256]{2,1,0:T(8,128)(2,1)}), bf16[8,1968,256]{2,1,0:T(8,128)(2,1)}, u32[]{:S(2)}, u32[]{:S(2)}) %all-to-all-start.5) | async-done | bytes 8060960 | tf_op jit(solution)/shard_map/all_to_all | solution.py:66
  292.8 7.7 %copy.76 = bf16[8,246,8,256]{3,2,0,1:T(8,128)(2,1)} copy(bf16[8,246,8,256]{3,2,1,0:T(8,128)(2,1)} %bitcast.9) | data formatting | bytes 16121856 | tf_op jit(solution)/shard_map/reshape | solution.py:65
  300.5 5.6 %fusion.3 = (f32[256]{0:T(256)S(1)}, f32[256,1968]{0,1:T(8,128)S(1)}) fusion(bf16[256,2048]{1,0:T(8,128)(2,1)S(1)} %copy-done.3, bf16[1968,2048]{1,0:T(8,128)(2,1)} %bitcast.19), kind=kOutput, calls=%fused_computation.39 | convolution fusion | flops 2064101120 | bytes 11125760 | tf_op jit(solution)/shard_map/dot_general | solution.py:19
  306.3 1.0 exponential_reduce_fusion
  308.0 0.9 copy.73
  308.9 9.9 %all-to-all-start.6 = ((f32[64,4,2,4]{1,3,2,0:T(4,128)}), f32[64,4,2,4]{1,3,2,0:T(4,128)S(1)}, u32[]{:S(2)}, u32[]{:S(2)}) async-start(f32[64,4,2,4]{1,3,2,0:T(4,128)} %copy.73), calls=%async_computation.6 | async-start | bytes 524288 | tf_op jit(solution)/shard_map/all_to_all | solution.py:87
  319.4 21.7 %all-to-all-done.6 = f32[64,4,2,4]{1,3,2,0:T(4,128)S(1)} async-done(((f32[64,4,2,4]{1,3,2,0:T(4,128)}), f32[64,4,2,4]{1,3,2,0:T(4,128)S(1)}, u32[]{:S(2)}, u32[]{:S(2)}) %all-to-all-start.6) | async-done | bytes 8224 | tf_op jit(solution)/shard_map/all_to_all | solution.py:87
  341.2 1.0 copy.74
  342.2 0.6 slice_reduce_fusion
  343.1 0.6 subtract_select_fusion
  343.7 0.5 subtract_select_fusion.1
  (48 shorter events, 2.8 us)
Async XLA Ops:
  0.6 1.1 copy-start
  3.1 53.2 %copy-start.4 = (f32[2048]{0:T(1024)S(1)}, f32[2048]{0:T(1024)}, u32[]{:S(2)}) copy-start(f32[2048]{0:T(1024)} %param.10) | copy-start | bytes 24580
  3.1 53.2 %copy-start.5 = (f32[2048]{0:T(1024)S(1)}, f32[2048]{0:T(1024)}, u32[]{:S(2)}) copy-start(f32[2048]{0:T(1024)} %param.9) | copy-start | bytes 24580
  80.4 14.5 %slice-start = ((bf16[3920,256]{1,0:T(8,128)(2,1)}), bf16[1952,256]{1,0:T(8,128)(2,1)S(1)}, s32[]{:S(2)}) async-start(bf16[3920,256]{1,0:T(8,128)(2,1)} %param.11), calls=%async_computation.7 | async-start | bytes 1998848 | tf_op jit(solution)/shard_map/slice | solution.py:66
  80.4 14.5 %all-to-all-start.3 = ((bf16[4,16,4,2048]{3,2,1,0:T(4,128)(2,1)}), bf16[4,16,4,2048]{3,2,1,0:T(4,128)(2,1)S(1)}, u32[]{:S(2)}, u32[]{:S(2)}) async-start(bf16[4,16,4,2048]{3,2,1,0:T(4,128)(2,1)} %broadcast_in_dim.27), calls=%async_computation.3 | async-start | bytes 2097152 | tf_op jit(solution)/shard_map/all_to_all | solution.py:50
  98.6 94.4 %all-to-all-start.4 = ((bf16[8,1952,256]{2,1,0:T(8,128)(2,1)}), bf16[8,1952,256]{2,1,0:T(8,128)(2,1)}, u32[]{:S(2)}, u32[]{:S(2)}) async-start(bf16[8,1952,256]{2,1,0:T(8,128)(2,1)} %stack.26), calls=%async_computation.4 | async-start | bytes 15990784 | tf_op jit(solution)/shard_map/all_to_all | solution.py:66
  103.9 89.1 %slice-start.1 = ((bf16[3920,256]{1,0:T(8,128)(2,1)}), bf16[1968,256]{1,0:T(8,128)(2,1)S(1)}, s32[]{:S(2)}) async-start(bf16[3920,256]{1,0:T(8,128)(2,1)} %param.11), calls=%async_computation.8 | async-start | bytes 2015232 | tf_op jit(solution)/shard_map/slice | solution.py:66
  196.7 6.4 %copy-start.7 = (s32[256]{0:T(256)S(1)}, s32[256]{0:T(256)}, u32[]{:S(2)}) copy-start(s32[256]{0:T(256)} %param.14) | copy-start | bytes 3076
  196.7 96.1 %all-to-all-start.5 = ((bf16[8,1968,256]{2,1,0:T(8,128)(2,1)}), bf16[8,1968,256]{2,1,0:T(8,128)(2,1)}, u32[]{:S(2)}, u32[]{:S(2)}) async-start(bf16[8,1968,256]{2,1,0:T(8,128)(2,1)} %stack.63), calls=%async_computation.5 | async-start | bytes 16121856 | tf_op jit(solution)/shard_map/all_to_all | solution.py:66
  204.8 7.7 %copy-start.2 = (bf16[256,2048]{1,0:T(8,128)(2,1)S(1)}, bf16[256,2048]{1,0:T(8,128)(2,1)}, u32[]{:S(2)}) copy-start(bf16[256,2048]{1,0:T(8,128)(2,1)} %reshape.142) | copy-start | bytes 3145732
  292.8 7.7 %copy-start.3 = (bf16[256,2048]{1,0:T(8,128)(2,1)S(1)}, bf16[256,2048]{1,0:T(8,128)(2,1)}, u32[]{:S(2)}) copy-start(bf16[256,2048]{1,0:T(8,128)(2,1)} %reshape.142) | copy-start | bytes 3145732
  306.3 37.9 %copy-start.1 = (bf16[128,2048]{1,0:T(8,128)(2,1)S(1)}, bf16[128,2048]{1,0:T(8,128)(2,1)}, u32[]{:S(2)}) copy-start(bf16[128,2048]{1,0:T(8,128)(2,1)} %param.8) | copy-start | bytes 1572868
  306.3 36.8 %copy-start.6 = (s32[256]{0:T(256)S(1)}, s32[256]{0:T(256)}, u32[]{:S(2)}) copy-start(s32[256]{0:T(256)} %param.13) | copy-start | bytes 3076
  306.3 36.8 %copy-start.8 = (s32[256]{0:T(256)S(1)}, s32[256]{0:T(256)}, u32[]{:S(2)}) copy-start(s32[256]{0:T(256)} %param.15) | copy-start | bytes 3076
  308.9 32.3 %all-to-all-start.6 = ((f32[64,4,2,4]{1,3,2,0:T(4,128)}), f32[64,4,2,4]{1,3,2,0:T(4,128)S(1)}, u32[]{:S(2)}, u32[]{:S(2)}) async-start(f32[64,4,2,4]{1,3,2,0:T(4,128)} %copy.73), calls=%async_computation.6 | async-start | bytes 524288 | tf_op jit(solution)/shard_map/all_to_all | solution.py:87
